TPU v7x, 32 devices: a whole 2x2x4 slice. The times are simulated.
32 devices in a mesh: groups: 2 (over y), expert: 4 (over z), dp: 4 (over x, core).
Axes of the slice: x: 2, y: 2, z: 4, core: 2. Of those that a mesh axis runs over, the one named last changes fastest.
Arguments:
- out_grad: bfloat16 [4096, 2048], P(('groups', 'expert', 'dp')), parts along dimension 0, may hold values from -0.5 to 0.5
- gate_weights: bfloat16 [4096, 8], P(('groups', 'expert', 'dp')), parts along dimension 0, may hold values from 0.049804688 to 0.5
- expert_ids: int32 [4096, 8], P(('groups', 'expert', 'dp')), parts along dimension 0, may hold values from 0 to 31, all different within a row; in each aligned block of 128 rows (0 to 127, 128 to 255, ...) at most 36 rows name the same one
- hidden: bfloat16 [32, 8, 4, 36, 768], P('expert', ('groups', 'dp')), parts along dimension 1, may hold values from -6 to 6
- down_weight: bfloat16 [32, 768, 2048], P('expert', None, 'dp'), may hold values from -0.21875 to 0.21875
Outputs:
- weight_grad: float32 [64, 768, 2048], P(('groups', 'expert'), None, 'dp'), parts along dimension 0
- gate_grad: float32 [4096, 8], P(('groups', 'expert', 'dp')), parts along dimension 0
There are 2 independent parts, one for each index of `groups`. A program takes and returns all parts, laid end to end along the dimension named above; an argument that names none is the same for every part. Nothing has to cross between parts.
Inputs may be any that keep to these rules, and one draw needn't show every extreme that they name: `expert_ids`: each token names 8 different experts; within each block of 128 tokens (one device's tokens) no expert is named by more than 36 tokens, a bound that some block reaches.
All inputs are finite; a program needn't handle non-finite values.
Results may differ from a plain program's by a relative error of at most 0.0095.
Values may be sent and summed in bfloat16 or wider, within the bound.
No kernel may reach another device: no remote copies, remote signals or barrier semaphores. Data moves between devices by JAX's collectives and lax.ppermute only.
A program may use at most 128 MiB of HBM per device.

v0:
```python
import jax
import jax.numpy as jnp
from jax import lax
from jax.sharding import PartitionSpec as P


def per_device(out_grad, gate_weights, expert_ids, hidden, down_weight):
    tok_rows, top_count = expert_ids.shape
    row_width = out_grad.shape[1]
    local_count = hidden.shape[0]
    capacity = hidden.shape[3]
    peer_count = lax.axis_size("expert")
    shards = lax.axis_size("dp")
    expert_count = local_count * peer_count
    col_width = row_width // shards
    block_count = peer_count * shards
    f32 = jnp.float32
    bf16 = jnp.bfloat16
    my_dp = lax.axis_index("dp")
    fetched = lax.ppermute(hidden, "dp", [(j, j ^ 2) for j in range(shards)])
    paired = lax.ppermute(
        jnp.concatenate([hidden, fetched], axis=1), "dp", [(j, j ^ 1) for j in range(shards)]
    )
    pieces = [hidden, fetched, paired[:, 0:1], paired[:, 1:2]]
    piece_replica = [my_dp, my_dp ^ 2, my_dp ^ 1, my_dp ^ 3]
    meta = jnp.concatenate([expert_ids.astype(bf16), gate_weights], axis=1).reshape(-1)
    meta_len = meta.shape[0]
    meta_rows = -(-meta_len // col_width)
    meta = jnp.pad(meta, (0, meta_rows * col_width - meta_len)).reshape(meta_rows, 1, col_width)
    cols = out_grad.reshape(tok_rows, shards, col_width)
    cols = jnp.concatenate([cols, jnp.broadcast_to(meta, (meta_rows, shards, col_width))], axis=0)
    cols = lax.all_to_all(cols, "dp", split_axis=1, concat_axis=0, tiled=True)
    cols = cols.reshape(shards, tok_rows + meta_rows, col_width)
    got = lax.all_gather(cols, "expert", axis=0, tiled=False)
    got = got.reshape(block_count, tok_rows + meta_rows, col_width)
    grad_all = got[:, :tok_rows]
    meta_all = got[:, tok_rows:].reshape(block_count, meta_rows * col_width)[:, :meta_len]
    meta_all = meta_all.reshape(block_count, tok_rows, 2 * top_count)
    ids_all = meta_all[:, :, :top_count].astype(jnp.int32)
    gate_all = meta_all[:, :, top_count:]
    my_experts = lax.axis_index("expert") * local_count + jnp.arange(local_count, dtype=jnp.int32)
    hit = ids_all[:, :, :, None] == my_experts[None, None, None, :]
    chose = jnp.any(hit, axis=2)
    gate_hit = jnp.sum(jnp.where(hit, gate_all.astype(f32)[:, :, :, None], 0.0), axis=2)
    before = (jnp.arange(tok_rows)[:, None] < jnp.arange(tok_rows)[None, :]).astype(bf16)
    rank = jnp.einsum("bul,ut->btl", chose.astype(bf16), before, preferred_element_type=f32).astype(
        jnp.int32
    )
    slot_ids = jnp.arange(capacity, dtype=jnp.int32)
    chose_t = chose.transpose(0, 2, 1)
    rank_t = rank.transpose(0, 2, 1)
    gate_t = gate_hit.transpose(0, 2, 1)
    select = chose_t[:, :, None, :] & (rank_t[:, :, None, :] == slot_ids[None, None, :, None])
    select_gate = jnp.where(select, gate_t[:, :, None, :], 0.0).astype(bf16)
    grad_rows = jnp.einsum(
        "blct,btd->blcd", select.astype(bf16), grad_all, preferred_element_type=f32
    ).astype(bf16)
    scaled = jnp.einsum("blct,btd->blcd", select_gate, grad_all, preferred_element_type=f32).astype(
        bf16
    )
    grad_rows = grad_rows.reshape(peer_count, shards, local_count, capacity, col_width)
    scaled = scaled.reshape(peer_count, shards, local_count, capacity, col_width)
    weight_grad = None
    slot_part = jnp.zeros((peer_count, shards, local_count, capacity), f32)
    for piece, replica in zip(pieces, piece_replica):
        piece = piece[:, 0]
        scaled_r = lax.dynamic_index_in_dim(scaled, replica, axis=1, keepdims=False)
        rows_r = lax.dynamic_index_in_dim(grad_rows, replica, axis=1, keepdims=False)
        part = (
            jnp.einsum("lscf,slcd->lfd", piece, scaled_r, preferred_element_type=f32)
            .astype(bf16)
            .astype(f32)
        )
        weight_grad = part if weight_grad is None else weight_grad + part
        expert_out = jnp.einsum("lscf,lfd->slcd", piece, down_weight, preferred_element_type=f32)
        slot_r = jnp.sum(rows_r.astype(f32) * expert_out, axis=3)
        slot_part = lax.dynamic_update_index_in_dim(slot_part, slot_r, replica, axis=1)
    send_back = slot_part.reshape(block_count, local_count, capacity)
    returned = lax.all_to_all(send_back, ("expert", "dp"), split_axis=0, concat_axis=0, tiled=True)
    returned = returned.reshape(peer_count, shards, local_count, capacity)
    slot_grad = jnp.sum(returned, axis=1).reshape(expert_count, capacity)
    own_hit = expert_ids[:, :, None] == jnp.arange(expert_count, dtype=jnp.int32)[None, None, :]
    own_chose = jnp.any(own_hit, axis=1)
    own_rank = jnp.einsum(
        "ue,ut->te", own_chose.astype(bf16), before, preferred_element_type=f32
    ).astype(jnp.int32)
    own_slot = jnp.sum(jnp.where(own_hit, own_rank[:, None, :], 0), axis=2)
    by_slot = jnp.sum(jnp.where(own_hit[:, :, :, None], slot_grad[None, None], 0.0), axis=2)
    gate_grad = jnp.sum(
        jnp.where(own_slot[:, :, None] == slot_ids[None, None, :], by_slot, 0.0), axis=2
    )
    return (weight_grad, gate_grad)


def solution(mesh):
    return jax.shard_map(
        per_device,
        mesh=mesh,
        in_specs=(
            P(("groups", "expert", "dp"), None),
            P(("groups", "expert", "dp"), None),
            P(("groups", "expert", "dp"), None),
            P("expert", ("groups", "dp"), None, None, None),
            P("expert", None, "dp"),
        ),
        out_specs=(P(("groups", "expert"), None, "dp"), P(("groups", "expert", "dp"), None)),
        check_vma=False,
    )
```

profile of v0, /device:TPU:0, one launch (start us, length us, event | category | flops | bytes accessed | tf_op | source)
XLA Modules:
  0.0 151.6 jit_solution(17778870522974405558)
XLA Ops:
  9.0 1.3 copy.186
  11.1 13.3 %all_to_all.20 = bf16[132,4,512]{2,0,1:T(8,128)(2,1)} all-to-all(bf16[132,4,512]{2,0,1:T(8,128)(2,1)S(1)} %copy.189), channel_id=1, replica_groups=mesh['groups'=2,'expert'=4,'dp'=4] {'dp'}, dimensions={1} | all-to-all | bytes 1081344 | tf_op jit(solution)/shard_map/all_to_all | solution.py:32
  24.4 2.0 %copy.196 = bf16[8,1,4,36,768]{4,0,3,2,1:T(8,128)(2,1)S(1)} copy(bf16[8,1,4,36,768]{4,2,3,1,0:T(4,128)(2,1)} %param.8) | data formatting | bytes 3538944 | tf_op args[3]
  27.7 39.3 %collective-permute-done = bf16[8,1,4,36,768]{4,0,3,2,1:T(8,128)(2,1)S(1)} collective-permute-done((bf16[8,1,4,36,768]{4,0,3,2,1:T(8,128)(2,1)S(1)}, bf16[8,1,4,36,768]{4,0,3,2,1:T(8,128)(2,1)S(1)}, u32[]{:S(2)}, u32[]{:S(2)}) %collective-permute-start) | collective-permute-done | bytes 1769504 | tf_op jit(solution)/shard_map/ppermute | solution.py:20
  67.0 2.3 %pad_maximum_fusion = bf16[8,2,4,36,768]{4,0,3,2,1:T(8,128)(2,1)} fusion(bf16[8,1,4,36,768]{4,0,3,2,1:T(8,128)(2,1)S(1)} %collective-permute-done, bf16[8,1,4,36,768]{4,0,3,2,1:T(8,128)(2,1)S(1)} %copy.196), kind=kLoop, calls=%fused_computation.15 | loop fusion | flops 1769472 | bytes 7077888 | tf_op jit(solution)/shard_map/concatenate | solution.py:22
  69.3 4.3 %all-gather.3.cloned.1.call-done = bf16[16,132,1,512]{3,1,2,0:T(8,128)(2,1)} async-done(((bf16[4,132,1,512]{3,1,2,0:T(8,128)(2,1)}), bf16[16,132,1,512]{3,1,2,0:T(8,128)(2,1)}) %all-gather.3.cloned.1.call-update) | async-done | bytes 2162704 | tf_op jit(solution)/shard_map/all_gather | solution.py:34
  75.0 1.0 fusion.56
  76.0 1.2 copy.226
  77.9 1.5 convolution_convert_fusion.1
  79.5 1.5 %convolution_convert_fusion = bf16[16,8,36,512]{3,2,1,0:T(8,128)(2,1)S(1)} fusion(bf16[16,132,512]{2,1,0:T(8,128)(2,1)S(1)} %bitcast.135, bf16[16,8,128]{2,1,0:T(8,128)(2,1)S(1)} %bitcast.142, s32[16,8,128]{2,1,0:T(8,128)S(1)} %convolution_convert_fusion.2, pred[16,8,128]{2,1,0:T(8,128)(4,1)S(1)} %bitcast.141), kind=kOutput, calls=%fused_computation.16 | convolution fusion | flops 608108544 | bytes 6930432 | tf_op jit(solution)/shard_map/blct,btd->blcd/dot_general | solution.py:58
  81.0 4.1 %constant_dynamic-slice_fusion = (bf16[4,1,8,36,512]{4,3,2,1,0:T(8,128)(2,1)}, bf16[4,1,8,36,512]{4,3,2,1,0:T(8,128)(2,1)}, bf16[4,1,8,36,512]{4,3,2,1,0:T(8,128...) fusion(bf16[4,4,8,36,512]{4,3,2,1,0:T(8,128)(2,1)S(1)} %bitcast, ...), kind=kLoop, calls=%fused_computation.78 | loop fusion | bytes 18874384 | tf_op jit(solution)/shard_map/jit(dynamic_index_in_dim)/dynamic_slice | solution.py:68
  85.1 5.0 %fusion.12 = f32[4,8,36]{2,0,1:T(4,128)S(1)} fusion(bf16[4,1,8,36,512]{4,3,2,1,0:T(8,128)(2,1)} %get-tuple-element.21, bf16[8,4,36,768]{3,1,2,0:T(4,128)(2,1)} %bitcast.138, bf16[8,768,512]{2,1,0:T(8,128)(2,1)} %param.9), kind=kOutput, calls=%fused_computation.25 | convolution fusion | flops 907737984 | bytes 9245184 | tf_op jit(solution)/shard_map/lscf,lfd->slcd/dot_general | solution.py:75
  91.4 4.3 %fusion.11 = f32[4,8,36]{2,0,1:T(4,128)S(1)} fusion(bf16[4,1,8,36,512]{4,3,2,1,0:T(8,128)(2,1)S(1)} %copy-done.10, bf16[8,1,4,36,768]{4,0,3,2,1:T(8,128)(2,1)S(1)} %copy-done.4, bf16[8,768,512]{2,1,0:T(8,128)(2,1)} %param.9), kind=kOutput, calls=%fused_computation.23 | convolution fusion | flops 907737984 | bytes 9245184 | tf_op jit(solution)/shard_map/lscf,lfd->slcd/dot_general | solution.py:75
  96.4 4.6 %fusion.22 = bf16[8,512,768,1]{2,1,3,0:T(8,128)(2,1)} fusion(bf16[8,4,36,768]{3,1,2,0:T(4,128)(2,1)S(1)} %bitcast.139, bf16[4,1,8,36,512]{4,3,2,1,0:T(8,128)(2,1)S(1)} %copy-done.9), kind=kOutput, calls=%fused_computation.39 | convolution fusion | flops 905969664 | bytes 9240576 | tf_op jit(solution)/shard_map/lscf,slcd->lfd/dot_general | solution.py:70
  101.0 2.3 %fusion.55 = (bf16[8,1,4,36,768]{4,0,3,2,1:T(8,128)(2,1)S(1)}, bf16[8,1,4,36,768]{4,0,3,2,1:T(8,128)(2,1)S(1)}) fusion(bf16[8,2,4,36,768]{4,0,3,2,1:T(8,128)(2,1)} %collective-permute-done.1), kind=kLoop, calls=%fused_computation.88 | loop fusion | bytes 7077888 | tf_op jit(solution)/shard_map/slice | solution.py:24
  103.4 1.6 %fusion.9 = f32[4,8,36]{2,0,1:T(4,128)S(1)} fusion(bf16[4,1,8,36,512]{4,3,2,1,0:T(8,128)(2,1)S(1)} %copy-done.8, bf16[8,768,512]{2,1,0:T(8,128)(2,1)S(1)} %bitcast.149, bf16[8,1,4,36,768]{4,0,3,2,1:T(8,128)(2,1)S(1)} %get-tuple-element.26), kind=kOutput, calls=%fused_computation.19 | convolution fusion | flops 907737984 | bytes 9245184 | tf_op jit(solution)/shard_map/lscf,lfd->slcd/dot_general | solution.py:75
  105.0 1.8 %fusion.10 = f32[4,8,36]{2,0,1:T(4,128)S(1)} fusion(bf16[4,1,8,36,512]{4,3,2,1,0:T(8,128)(2,1)S(1)} %copy-done.7, bf16[8,768,512]{2,1,0:T(8,128)(2,1)S(1)} %bitcast.149, bf16[8,1,4,36,768]{4,0,3,2,1:T(8,128)(2,1)S(1)} %get-tuple-element.27), kind=kOutput, calls=%fused_computation.21 | convolution fusion | flops 907737984 | bytes 9245184 | tf_op jit(solution)/shard_map/lscf,lfd->slcd/dot_general | solution.py:75
  108.0 1.6 %reshape.70 = f32[16,1,288]{2,1,0:T(1,128)} reshape(f32[16,8,36]{2,1,0:T(8,128)} %bitcast.43) | data formatting | bytes 36864
  109.5 4.1 %all-to-all-start.1 = ((f32[16,1,288]{2,1,0:T(1,128)}), f32[16,1,288]{2,1,0:T(1,128)}, u32[]{:S(2)}, u32[]{:S(2)}) async-start(f32[16,1,288]{2,1,0:T(1,128)} %reshape.70), calls=%async_computation.1 | async-start | bytes 49152 | tf_op jit(solution)/shard_map/all_to_all | solution.py:79
  113.7 3.4 %fusion.17 = bf16[8,768,512,1]{1,2,3,0:T(8,128)(2,1)S(1)} fusion(bf16[8,1,4,36,768]{4,0,3,2,1:T(8,128)(2,1)S(1)} %get-tuple-element.27, bf16[4,1,8,36,512]{4,3,2,1,0:T(8,128)(2,1)} %get-tuple-element.33), kind=kOutput, calls=%fused_computation.34 | convolution fusion | flops 905969664 | bytes 9240576 | tf_op jit(solution)/shard_map/lscf,slcd->lfd/dot_general | solution.py:70
  117.1 1.9 %fusion.18 = bf16[8,768,512,1]{1,2,3,0:T(8,128)(2,1)S(1)} fusion(bf16[8,1,4,36,768]{4,0,3,2,1:T(8,128)(2,1)S(1)} %get-tuple-element.26, bf16[4,1,8,36,512]{4,3,2,1,0:T(8,128)(2,1)S(1)} %copy-done), kind=kOutput, calls=%fused_computation.35 | convolution fusion | flops 905969664 | bytes 9240576 | tf_op jit(solution)/shard_map/lscf,slcd->lfd/dot_general | solution.py:70
  119.0 9.5 %fusion = f32[8,768,512]{1,2,0:T(8,128)} fusion(bf16[8,512,768,1]{2,1,3,0:T(8,128)(2,1)} %fusion.22, bf16[8,768,512,1]{1,2,3,0:T(8,128)(2,1)S(1)} %fusion.17, bf16[8,768,512,1]{1,2,3,0:T(8,128)(2,1)S(1)} %fusion.18, bf16[8,1,4,36,768]{4,0,3,2,1:T(8,128)(2,1)S(1)} %copy-done.5, bf16[4,1,8,36,512]{4,3,2,1,0:T(8,128)(2,1)} %get-tuple-element.35), kind=kOutput, calls=%fused_computation.3 | convolution fusion | flops 931135488 | bytes 34406400 | tf_op jit(solution)/shard_map/lscf,slcd->lfd/dot_general | solution.py:70
  128.5 12.6 %copy.216 = f32[8,768,512]{2,1,0:T(8,128)} copy(f32[8,768,512]{1,2,0:T(8,128)} %fusion) | data formatting | bytes 25165824
  141.6 1.4 reduce
  (68 shorter events, 11.2 us)
Async XLA Ops:
  7.2 66.5 %all-gather.3.cloned.1.call-start = ((), (), s32[]{:S(2)}) async-start(), calls=%async_computation.2 | async-start | bytes 2785280 | tf_op jit(solution)/shard_map/all_gather | solution.py:34
  24.4 2.5 %copy-start.12 = (s32[128,8]{0,1:T(8,128)S(1)}, s32[128,8]{0,1:T(8,128)}, u32[]{:S(2)}) copy-start(s32[128,8]{0,1:T(8,128)} %param.7) | copy-start | bytes 12292
  26.4 40.5 %collective-permute-start = (bf16[8,1,4,36,768]{4,0,3,2,1:T(8,128)(2,1)S(1)}, bf16[8,1,4,36,768]{4,0,3,2,1:T(8,128)(2,1)S(1)}, u32[]{:S(2)}, u32[]{:S(2)}) collective-permute-start(bf16[8,1,4,36,768]{4,0,3,2,1:T(8,128)(2,1)S(1)} %copy.196), channel_id=1, source_target_pairs={{0,2},{1,3},{2,0},{3,1},{4,6},{5,7},{6,4},{7,5},{8,10},{9,11},{10,... | collective-permute-start | bytes 5308424 | tf_op jit(solution)/shard_map/ppermute | solution.py:20
  67.0 2.4 %copy-start.3 = (bf16[8,1,4,36,768]{4,0,3,2,1:T(8,128)(2,1)}, bf16[8,1,4,36,768]{4,0,3,2,1:T(8,128)(2,1)S(1)}, u32[]{:S(2)}) copy-start(bf16[8,1,4,36,768]{4,0,3,2,1:T(8,128)(2,1)S(1)} %collective-permute-done) | copy-start | bytes 5308420
  69.3 31.7 %collective-permute-start.1 = (bf16[8,2,4,36,768]{4,0,3,2,1:T(8,128)(2,1)}, bf16[8,2,4,36,768]{4,0,3,2,1:T(8,128)(2,1)}, u32[]{:S(2)}, u32[]{:S(2)}) collective-permute-start(bf16[8,2,4,36,768]{4,0,3,2,1:T(8,128)(2,1)} %pad_maximum_fusion), channel_id=1, source_target_pairs={{0,1},{1,0},{2,3},{3,2},{4,5},{5,4},{6,7},{7,6},{8,9},{9,8},{10,11... | collective-permute-start | bytes 10616840 | tf_op jit(solution)/shard_map/ppermute | solution.py:21
  75.0 2.9 %copy-start.1 = (bf16[16,132,1,512]{3,1,2,0:T(8,128)(2,1)S(1)}, bf16[16,132,1,512]{3,1,2,0:T(8,128)(2,1)}, u32[]{:S(2)}) copy-start(bf16[16,132,1,512]{3,1,2,0:T(8,128)(2,1)} %all-gather.3.cloned.1.call-done) | copy-start | bytes 6488068
  77.9 1.6 %copy-start.2 = (bf16[16,132,1,512]{3,1,2,0:T(8,128)(2,1)S(1)}, bf16[16,132,1,512]{3,1,2,0:T(8,128)(2,1)}, u32[]{:S(2)}) copy-start(bf16[16,132,1,512]{3,1,2,0:T(8,128)(2,1)} %all-gather.3.cloned.1.call-done) | copy-start | bytes 6488068
  85.1 6.3 %copy-start.4 = (bf16[8,1,4,36,768]{4,0,3,2,1:T(8,128)(2,1)S(1)}, bf16[8,1,4,36,768]{4,0,3,2,1:T(8,128)(2,1)}, u32[]{:S(2)}) copy-start(bf16[8,1,4,36,768]{4,0,3,2,1:T(8,128)(2,1)} %copy-done.3) | copy-start | bytes 5308420
  85.1 6.3 %copy-start.10 = (bf16[4,1,8,36,512]{4,3,2,1,0:T(8,128)(2,1)S(1)}, bf16[4,1,8,36,512]{4,3,2,1,0:T(8,128)(2,1)}, u32[]{:S(2)}) copy-start(bf16[4,1,8,36,512]{4,3,2,1,0:T(8,128)(2,1)} %get-tuple-element.20) | copy-start | bytes 3538948
  91.4 5.0 %copy-start.6 = (bf16[8,1,4,36,768]{4,2,3,1,0:T(4,128)(2,1)S(1)}, bf16[8,1,4,36,768]{4,2,3,1,0:T(4,128)(2,1)}, u32[]{:S(2)}) copy-start(bf16[8,1,4,36,768]{4,2,3,1,0:T(4,128)(2,1)} %param.8) | copy-start | bytes 5308420
  91.4 5.0 %copy-start.9 = (bf16[4,1,8,36,512]{4,3,2,1,0:T(8,128)(2,1)S(1)}, bf16[4,1,8,36,512]{4,3,2,1,0:T(8,128)(2,1)}, u32[]{:S(2)}) copy-start(bf16[4,1,8,36,512]{4,3,2,1,0:T(8,128)(2,1)} %get-tuple-element.32) | copy-start | bytes 3538948
  91.4 12.0 %slice-start = ((s8[6291456]{0:T(1024)(128)(4,1)}), s8[2097152]{0:T(1024)(128)(4,1)S(1)}, s32[]{:S(2)}) async-start(s8[6291456]{0:T(1024)(128)(4,1)} %bitcast.148), calls=%async_computation.3 | async-start | bytes 4194304
  96.4 7.0 %slice-start.1 = ((s8[6291456]{0:T(1024)(128)(4,1)}), s8[4194304]{0:T(1024)(128)(4,1)S(1)}, s32[]{:S(2)}) async-start(s8[6291456]{0:T(1024)(128)(4,1)} %bitcast.148), calls=%async_computation.4 | async-start | bytes 8388608
  101.0 2.4 %copy-start.8 = (bf16[4,1,8,36,512]{4,3,2,1,0:T(8,128)(2,1)S(1)}, bf16[4,1,8,36,512]{4,3,2,1,0:T(8,128)(2,1)}, u32[]{:S(2)}) copy-start(bf16[4,1,8,36,512]{4,3,2,1,0:T(8,128)(2,1)} %get-tuple-element.18) | copy-start | bytes 3538948
  103.4 1.6 %copy-start.7 = (bf16[4,1,8,36,512]{4,3,2,1,0:T(8,128)(2,1)S(1)}, bf16[4,1,8,36,512]{4,3,2,1,0:T(8,128)(2,1)}, u32[]{:S(2)}) copy-start(bf16[4,1,8,36,512]{4,3,2,1,0:T(8,128)(2,1)} %get-tuple-element.19) | copy-start | bytes 3538948
  109.5 31.6 %all-to-all-start.1 = ((f32[16,1,288]{2,1,0:T(1,128)}), f32[16,1,288]{2,1,0:T(1,128)}, u32[]{:S(2)}, u32[]{:S(2)}) async-start(f32[16,1,288]{2,1,0:T(1,128)} %reshape.70), calls=%async_computation.1 | async-start | bytes 49152 | tf_op jit(solution)/shard_map/all_to_all | solution.py:79
  113.7 3.4 %copy-start = (bf16[4,1,8,36,512]{4,3,2,1,0:T(8,128)(2,1)S(1)}, bf16[4,1,8,36,512]{4,3,2,1,0:T(8,128)(2,1)}, u32[]{:S(2)}) copy-start(bf16[4,1,8,36,512]{4,3,2,1,0:T(8,128)(2,1)} %get-tuple-element.34) | copy-start | bytes 3538948
  117.1 2.0 %copy-start.5 = (bf16[8,1,4,36,768]{4,0,3,2,1:T(8,128)(2,1)S(1)}, bf16[8,1,4,36,768]{4,0,3,2,1:T(8,128)(2,1)}, u32[]{:S(2)}) copy-start(bf16[8,1,4,36,768]{4,0,3,2,1:T(8,128)(2,1)} %copy-done.3) | copy-start | bytes 5308420
  128.5 14.8 %copy-start.11 = (pred[128,8,32]{0,2,1:T(8,128)(4,1)S(1)}, pred[128,8,32]{0,2,1:T(8,128)(4,1)}, u32[]{:S(2)}) copy-start(pred[128,8,32]{0,2,1:T(8,128)(4,1)} %get-tuple-element.31) | copy-start | bytes 98308
Sparse Core Ops, SparseCore 0:
  24.6 49.0 all-gather.2
where the time goes:
time: 152 us
  waiting for transfers between devices  43.6 us (29%)
  matrix products  35.5 us (23%)
  local copies, waits for them, and re-layouts  32.5 us (21%)
  between operations  14.3 us (9%)
  blocking collectives  13.3 us (9%)
  other arithmetic  7.75 us (5%)
  starting transfers between devices  4.59 us (3%)
    ppermute x1, waiting for transfers between devices, per_device(): fetched = lax.ppermute(hidden, 'dp', [(j, j ^ 2) for j in range(shards)])  39.3 us
    dot_general x4, matrix products, per_device(): jnp.einsum('lscf,slcd->lfd', piece, scaled_r, preferred_element_type=f32)  19.4 us
    unnamed x37, local copies, waits for them, and re-layouts  19.2 us
    all_to_all x1, blocking collectives, per_device(): cols = lax.all_to_all(cols, 'dp', split_axis=1, concat_axis=0, tiled=True)  13.3 us
    dot_general x4, matrix products, per_device(): jnp.einsum('lscf,lfd->slcd', piece, down_weight, preferred_element_type=f32)  12.7 us
    all_gather x1, waiting for transfers between devices, per_device(): got = lax.all_gather(cols, 'expert', axis=0, tiled=False)  4.34 us
    all_to_all x1, starting transfers between devices, per_device(): lax.all_to_all(send_back, ('expert', 'dp'), split_axis=0, concat_axis=0,...  4.13 us
    dynamic_slice x1, local copies, waits for them, and re-layouts, per_device(): lax.dynamic_index_in_dim(grad_rows, replica, axis=1, keepdims=False)  4.08 us
  transfers between devices with their start and end apart: 4, of which 2 were waited for; matrix products, arithmetic and copies ran while one was open for 39% of the time, Pallas kernels for 0%

commit v1 on v0

--- a/solution.py
+++ b/solution.py
@@ -2,6 +2,18 @@
 import jax.numpy as jnp
 from jax import lax
 from jax.sharding import PartitionSpec as P
+
+
+def split_up(x, dim, size):
+    lengths = x.shape
+    tiles = x.reshape(*lengths[:dim], size, lengths[dim] // size, *lengths[dim + 1 :])
+    return jnp.moveaxis(tiles, dim, 0)
+
+
+def in_order(blocks, dim):
+    dims = list(blocks.shape[1:])
+    dims[dim] *= blocks.shape[0]
+    return jnp.moveaxis(blocks, 0, dim).reshape(dims)
 
 
 def per_device(out_grad, gate_weights, expert_ids, hidden, down_weight):
@@ -29,7 +41,15 @@
     meta = jnp.pad(meta, (0, meta_rows * col_width - meta_len)).reshape(meta_rows, 1, col_width)
     cols = out_grad.reshape(tok_rows, shards, col_width)
     cols = jnp.concatenate([cols, jnp.broadcast_to(meta, (meta_rows, shards, col_width))], axis=0)
-    cols = lax.all_to_all(cols, "dp", split_axis=1, concat_axis=0, tiled=True)
+    devices, index = (lax.axis_size("dp"), lax.axis_index("dp"))
+    blocks = split_up(cols, 1, devices)
+    result = blocks
+    for step in range(1, devices):
+        target, source = ((index + step) % devices, (index - step) % devices)
+        sent = lax.dynamic_index_in_dim(blocks, target, 0)
+        other = lax.ppermute(sent, "dp", [(i, (i + step) % devices) for i in range(devices)])
+        result = lax.dynamic_update_slice_in_dim(result, other, source, axis=0)
+    cols = in_order(result, 0)
     cols = cols.reshape(shards, tok_rows + meta_rows, col_width)
     got = lax.all_gather(cols, "expert", axis=0, tiled=False)
     got = got.reshape(block_count, tok_rows + meta_rows, col_width)

time: 152 us -> 152 us (level)
  blocking collectives: 13.3 us -> 0 us
  starting transfers between devices: 4.59 us -> 10.1 us
  local copies, waits for them, and re-layouts: 32.5 us -> 35.3 us
  waiting for transfers between devices: 43.6 us -> 46.2 us
  matrix products: 35.5 us -> 37.1 us
    all_to_all x1 -> x0, blocking collectives: 13.3 us -> none  [per_device(): cols = lax.all_to_all(cols, 'dp', split_axis=1, concat_axis=0, tiled=True)]
    ppermute x0 -> x3, starting transfers between devices: none -> 4.84 us  [per_device(): lax.ppermute(sent, 'dp', [(i, (i + step) % devices) for i in range(device...]
    ppermute x0 -> x3, waiting for transfers between devices: none -> 3.78 us  [per_device(): lax.ppermute(sent, 'dp', [(i, (i + step) % devices) for i in range(device...]
    all_gather x0 -> x1, local copies, waits for them, and re-layouts: none -> 2.03 us  [per_device(): got = lax.all_gather(cols, 'expert', axis=0, tiled=False)]
    dot_general x1, matrix products: 1.52 us -> 3.13 us  [per_device(): jnp.einsum('blct,btd->blcd', select_gate, grad_all, preferred_element_typ...]
    unnamed x37 -> x35, local copies, waits for them, and re-layouts: 19.2 us -> 19.1 us
  transfers between devices with their start and end apart: 4 -> 7, of which waited for: 2 -> 4; matrix products, arithmetic and copies ran while one was open for 39% -> 42% of each run, Pallas kernels for 0% -> 0%
where the time goes in v1:
time: 152 us; the launch traced here: 151 us
  waiting for transfers between devices  46.2 us (30%)
  matrix products  37.1 us (24%)
  local copies, waits for them, and re-layouts  35.3 us (23%)
  between operations  14.4 us (9%)
  starting transfers between devices  10.1 us (7%)
  other arithmetic  7.92 us (5%)
    ppermute x1, waiting for transfers between devices, per_device(): fetched = lax.ppermute(hidden, 'dp', [(j, j ^ 2) for j in range(shards)])  38.8 us
    dot_general x4, matrix products, per_device(): jnp.einsum('lscf,slcd->lfd', piece, scaled_r, preferred_element_type=f32)  19.4 us
    unnamed x35, local copies, waits for them, and re-layouts  19.1 us
    dot_general x4, matrix products, per_device(): jnp.einsum('lscf,lfd->slcd', piece, down_weight, preferred_element_type=f32)  12.7 us
    ppermute x3, starting transfers between devices, per_device(): lax.ppermute(sent, 'dp', [(i, (i + step) % devices) for i in range(device...  4.84 us
    all_to_all x1, starting transfers between devices, per_device(): lax.all_to_all(send_back, ('expert', 'dp'), split_axis=0, concat_axis=0,...  4.13 us
    dynamic_slice x1, local copies, waits for them, and re-layouts, per_device(): lax.dynamic_index_in_dim(grad_rows, replica, axis=1, keepdims=False)  4.08 us
    ppermute x3, waiting for transfers between devices, per_device(): lax.ppermute(sent, 'dp', [(i, (i + step) % devices) for i in range(device...  3.78 us
  transfers between devices with their start and end apart: 7, of which 4 were waited for; matrix products, arithmetic and copies ran while one was open for 42% of the time, Pallas kernels for 0%

profile of v1, /device:TPU:0, one launch (start us, length us, event | category | flops | bytes accessed | tf_op | source)
XLA Modules:
  0.0 151.0 jit_solution(11275907401260138006)
XLA Ops:
  10.7 3.0 %collective-permute-start.1 = (bf16[1,132,1,512]{3,1,2,0:T(8,128)(2,1)S(1)}, bf16[1,132,1,512]{3,1,2,0:T(8,128)(2,1)S(1)}, u32[]{:S(2)}, u32[]{:S(2)}) collective-permute-start(bf16[1,132,1,512]{3,1,2,0:T(8,128)(2,1)S(1)} %bitcast.149), channel_id=1, source_target_pairs={{0,2},{1,3},{2,0},{3,1},{4,6},{5,7},{6,4},{7,5},{8,10},{9,11},{10,... | collective-permute-start | bytes 405512 | tf_op jit(solution)/shard_map/ppermute | solution.py:50
  14.0 1.8 %collective-permute-start.2 = (bf16[1,132,1,512]{3,1,2,0:T(8,128)(2,1)S(1)}, bf16[1,132,1,512]{3,1,2,0:T(8,128)(2,1)S(1)}, u32[]{:S(2)}, u32[]{:S(2)}) collective-permute-start(bf16[1,132,1,512]{3,1,2,0:T(8,128)(2,1)S(1)} %bitcast.153), channel_id=1, source_target_pairs={{0,3},{1,0},{2,1},{3,2},{4,7},{5,4},{6,5},{7,6},{8,11},{9,8},{10,9... | collective-permute-start | bytes 405512 | tf_op jit(solution)/shard_map/ppermute | solution.py:50
  16.0 1.8 %collective-permute-done.1 = bf16[1,132,1,512]{3,1,2,0:T(8,128)(2,1)S(1)} collective-permute-done((bf16[1,132,1,512]{3,1,2,0:T(8,128)(2,1)S(1)}, bf16[1,132,1,512]{3,1,2,0:T(8,128)(2,1)S(1)}, u32[]{:S(2)}, u32[]{:S(2)}) %collective-permute-start.1) | collective-permute-done | bytes 135200 | tf_op jit(solution)/shard_map/ppermute | solution.py:50
  18.0 1.9 %collective-permute-done = bf16[1,132,1,512]{3,1,2,0:T(8,128)(2,1)S(1)} collective-permute-done((bf16[1,132,1,512]{3,1,2,0:T(8,128)(2,1)S(1)}, bf16[1,132,1,512]{3,1,2,0:T(8,128)(2,1)S(1)}, u32[]{:S(2)}, u32[]{:S(2)}) %collective-permute-start) | collective-permute-done | bytes 135200 | tf_op jit(solution)/shard_map/ppermute | solution.py:50
  21.7 2.0 %copy.217 = bf16[8,1,4,36,768]{4,0,3,2,1:T(8,128)(2,1)S(1)} copy(bf16[8,1,4,36,768]{4,2,3,1,0:T(4,128)(2,1)} %param.8) | data formatting | bytes 3538944 | tf_op args[3]
  25.6 38.8 %collective-permute-done.3 = bf16[8,1,4,36,768]{4,0,3,2,1:T(8,128)(2,1)S(1)} collective-permute-done((bf16[8,1,4,36,768]{4,0,3,2,1:T(8,128)(2,1)S(1)}, bf16[8,1,4,36,768]{4,0,3,2,1:T(8,128)(2,1)S(1)}, u32[]{:S(2)}, u32[]{:S(2)}) %collective-permute-start.3) | collective-permute-done | bytes 1769504 | tf_op jit(solution)/shard_map/ppermute | solution.py:32
  64.4 2.3 %pad_maximum_fusion = bf16[8,2,4,36,768]{4,0,3,2,1:T(8,128)(2,1)} fusion(bf16[8,1,4,36,768]{4,0,3,2,1:T(8,128)(2,1)S(1)} %collective-permute-done.3, bf16[8,1,4,36,768]{4,0,3,2,1:T(8,128)(2,1)S(1)} %copy.217), kind=kLoop, calls=%fused_computation.15 | loop fusion | flops 1769472 | bytes 7077888 | tf_op jit(solution)/shard_map/concatenate | solution.py:34
  66.7 3.6 %all-gather.2.cloned.1.call-done = bf16[4,4,132,512]{3,1,2,0:T(4,128)(2,1)} async-done(((bf16[1,4,132,512]{3,1,2,0:T(4,128)(2,1)}), bf16[4,4,132,512]{3,1,2,0:T(4,128)(2,1)}) %all-gather.2.cloned.1.call-update) | async-done | bytes 2162704 | tf_op jit(solution)/shard_map/all_gather | solution.py:54
  70.3 2.0 %copy.211 = bf16[4,4,132,512]{3,2,1,0:T(8,128)(2,1)S(1)} copy(bf16[4,4,132,512]{3,1,2,0:T(4,128)(2,1)} %all-gather.2.cloned.1.call-done) | data formatting | bytes 4325376 | tf_op jit(solution)/shard_map/all_gather | solution.py:54
  75.8 1.5 %convolution_convert_fusion.1 = bf16[16,8,36,512]{3,2,1,0:T(8,128)(2,1)S(1)} fusion(bf16[16,132,512]{2,1,0:T(8,128)(2,1)S(1)} %bitcast.141, s32[16,8,128]{2,1,0:T(8,128)S(1)} %convolution_convert_fusion.2, pred[16,8,128]{2,1,0:T(8,128)(4,1)S(1)} %bitcast.147), kind=kOutput, calls=%fused_computation.17 | convolution fusion | flops 607518720 | bytes 6897664 | tf_op jit(solution)/shard_map/blct,btd->blcd/dot_general | solution.py:75
  77.3 3.1 %convolution_convert_fusion = bf16[16,8,36,512]{3,2,1,0:T(8,128)(2,1)S(1)} fusion(bf16[16,132,512]{2,1,0:T(8,128)(2,1)} %bitcast.142, bf16[16,8,128]{2,1,0:T(8,128)(2,1)S(1)} %bitcast.155, s32[16,8,128]{2,1,0:T(8,128)S(1)} %convolution_convert_fusion.2, pred[16,8,128]{2,1,0:T(8,128)(4,1)S(1)} %bitcast.148), kind=kOutput, calls=%fused_computation.16 | convolution fusion | flops 608108544 | bytes 6930432 | tf_op jit(solution)/shard_map/blct,btd->blcd/dot_general | solution.py:78
  80.4 4.1 %constant_dynamic-slice_fusion = (bf16[4,1,8,36,512]{4,3,2,1,0:T(8,128)(2,1)}, bf16[4,1,8,36,512]{4,3,2,1,0:T(8,128)(2,1)}, bf16[4,1,8,36,512]{4,3,2,1,0:T(8,128...) fusion(bf16[4,4,8,36,512]{4,3,2,1,0:T(8,128)(2,1)S(1)} %bitcast, ...), kind=kLoop, calls=%fused_computation.87 | loop fusion | bytes 18874384 | tf_op jit(solution)/shard_map/jit(dynamic_index_in_dim)/dynamic_slice | solution.py:88
  84.5 5.0 %fusion.12 = f32[4,8,36]{2,0,1:T(4,128)S(1)} fusion(bf16[4,1,8,36,512]{4,3,2,1,0:T(8,128)(2,1)} %get-tuple-element.21, bf16[8,4,36,768]{3,1,2,0:T(4,128)(2,1)} %bitcast.145, bf16[8,768,512]{2,1,0:T(8,128)(2,1)} %param.9), kind=kOutput, calls=%fused_computation.25 | convolution fusion | flops 907737984 | bytes 9245184 | tf_op jit(solution)/shard_map/lscf,lfd->slcd/dot_general | solution.py:95
  90.8 4.3 %fusion.11 = f32[4,8,36]{2,0,1:T(4,128)S(1)} fusion(bf16[4,1,8,36,512]{4,3,2,1,0:T(8,128)(2,1)S(1)} %copy-done.9, bf16[8,1,4,36,768]{4,0,3,2,1:T(8,128)(2,1)S(1)} %copy-done.3, bf16[8,768,512]{2,1,0:T(8,128)(2,1)} %param.9), kind=kOutput, calls=%fused_computation.23 | convolution fusion | flops 907737984 | bytes 9245184 | tf_op jit(solution)/shard_map/lscf,lfd->slcd/dot_general | solution.py:95
  95.8 4.6 %fusion.22 = bf16[8,512,768,1]{2,1,3,0:T(8,128)(2,1)} fusion(bf16[8,4,36,768]{3,1,2,0:T(4,128)(2,1)S(1)} %bitcast.146, bf16[4,1,8,36,512]{4,3,2,1,0:T(8,128)(2,1)S(1)} %copy-done.8), kind=kOutput, calls=%fused_computation.43 | convolution fusion | flops 905969664 | bytes 9240576 | tf_op jit(solution)/shard_map/lscf,slcd->lfd/dot_general | solution.py:90
  100.4 2.3 %fusion.59 = (bf16[8,1,4,36,768]{4,0,3,2,1:T(8,128)(2,1)S(1)}, bf16[8,1,4,36,768]{4,0,3,2,1:T(8,128)(2,1)S(1)}) fusion(bf16[8,2,4,36,768]{4,0,3,2,1:T(8,128)(2,1)} %collective-permute-done.4), kind=kLoop, calls=%fused_computation.101 | loop fusion | bytes 7077888 | tf_op jit(solution)/shard_map/slice | solution.py:36
  102.8 1.7 %fusion.9 = f32[4,8,36]{2,0,1:T(4,128)S(1)} fusion(bf16[4,1,8,36,512]{4,3,2,1,0:T(8,128)(2,1)S(1)} %copy-done.7, bf16[8,768,512]{2,1,0:T(8,128)(2,1)S(1)} %bitcast.162, bf16[8,1,4,36,768]{4,0,3,2,1:T(8,128)(2,1)S(1)} %get-tuple-element.26), kind=kOutput, calls=%fused_computation.19 | convolution fusion | flops 907737984 | bytes 9245184 | tf_op jit(solution)/shard_map/lscf,lfd->slcd/dot_general | solution.py:95
  104.6 1.6 %fusion.10 = f32[4,8,36]{2,0,1:T(4,128)S(1)} fusion(bf16[4,1,8,36,512]{4,3,2,1,0:T(8,128)(2,1)S(1)} %copy-done.6, bf16[8,768,512]{2,1,0:T(8,128)(2,1)S(1)} %bitcast.162, bf16[8,1,4,36,768]{4,0,3,2,1:T(8,128)(2,1)S(1)} %get-tuple-element.27), kind=kOutput, calls=%fused_computation.21 | convolution fusion | flops 907737984 | bytes 9245184 | tf_op jit(solution)/shard_map/lscf,lfd->slcd/dot_general | solution.py:95
  107.4 1.6 %reshape.86 = f32[16,1,288]{2,1,0:T(1,128)} reshape(f32[16,8,36]{2,1,0:T(8,128)} %bitcast.49) | data formatting | bytes 36864
  109.0 4.1 %all-to-all-start = ((f32[16,1,288]{2,1,0:T(1,128)}), f32[16,1,288]{2,1,0:T(1,128)}, u32[]{:S(2)}, u32[]{:S(2)}) async-start(f32[16,1,288]{2,1,0:T(1,128)} %reshape.86), calls=%async_computation | async-start | bytes 49152 | tf_op jit(solution)/shard_map/all_to_all | solution.py:99
  113.1 3.4 %fusion.17 = bf16[8,768,512,1]{1,2,3,0:T(8,128)(2,1)S(1)} fusion(bf16[8,1,4,36,768]{4,0,3,2,1:T(8,128)(2,1)S(1)} %get-tuple-element.27, bf16[4,1,8,36,512]{4,3,2,1,0:T(8,128)(2,1)} %get-tuple-element.36), kind=kOutput, calls=%fused_computation.38 | convolution fusion | flops 905969664 | bytes 9240576 | tf_op jit(solution)/shard_map/lscf,slcd->lfd/dot_general | solution.py:90
  116.5 1.9 %fusion.18 = bf16[8,768,512,1]{1,2,3,0:T(8,128)(2,1)S(1)} fusion(bf16[8,1,4,36,768]{4,0,3,2,1:T(8,128)(2,1)S(1)} %get-tuple-element.26, bf16[4,1,8,36,512]{4,3,2,1,0:T(8,128)(2,1)S(1)} %copy-done.1), kind=kOutput, calls=%fused_computation.39 | convolution fusion | flops 905969664 | bytes 9240576 | tf_op jit(solution)/shard_map/lscf,slcd->lfd/dot_general | solution.py:90
  118.4 9.5 %fusion = f32[8,768,512]{1,2,0:T(8,128)} fusion(bf16[8,512,768,1]{2,1,3,0:T(8,128)(2,1)} %fusion.22, bf16[8,768,512,1]{1,2,3,0:T(8,128)(2,1)S(1)} %fusion.17, bf16[8,768,512,1]{1,2,3,0:T(8,128)(2,1)S(1)} %fusion.18, bf16[8,1,4,36,768]{4,0,3,2,1:T(8,128)(2,1)S(1)} %copy-done.4, bf16[4,1,8,36,512]{4,3,2,1,0:T(8,128)(2,1)} %get-tuple-element.38), kind=kOutput, calls=%fused_computation.3 | convolution fusion | flops 931135488 | bytes 34406400 | tf_op jit(solution)/shard_map/lscf,slcd->lfd/dot_general | solution.py:90
  127.9 12.6 %copy.237 = f32[8,768,512]{2,1,0:T(8,128)} copy(f32[8,768,512]{1,2,0:T(8,128)} %fusion) | data formatting | bytes 25165824
  (82 shorter events, 17.8 us)
Async XLA Ops:
  7.2 63.2 %all-gather.2.cloned.1.call-start = ((), (), s32[]{:S(2)}) async-start(), calls=%async_computation.1 | async-start | bytes 2703360 | tf_op jit(solution)/shard_map/all_gather | solution.py:54
  10.7 7.1 %collective-permute-start.1 = (bf16[1,132,1,512]{3,1,2,0:T(8,128)(2,1)S(1)}, bf16[1,132,1,512]{3,1,2,0:T(8,128)(2,1)S(1)}, u32[]{:S(2)}, u32[]{:S(2)}) collective-permute-start(bf16[1,132,1,512]{3,1,2,0:T(8,128)(2,1)S(1)} %bitcast.149), channel_id=1, source_target_pairs={{0,2},{1,3},{2,0},{3,1},{4,6},{5,7},{6,4},{7,5},{8,10},{9,11},{10,... | collective-permute-start | bytes 405512 | tf_op jit(solution)/shard_map/ppermute | solution.py:50
  13.9 6.1 %collective-permute-start = (bf16[1,132,1,512]{3,1,2,0:T(8,128)(2,1)S(1)}, bf16[1,132,1,512]{3,1,2,0:T(8,128)(2,1)S(1)}, u32[]{:S(2)}, u32[]{:S(2)}) collective-permute-start(bf16[1,132,1,512]{3,1,2,0:T(8,128)(2,1)S(1)} %bitcast.151), channel_id=1, source_target_pairs={{0,1},{1,2},{2,3},{3,0},{4,5},{5,6},{6,7},{7,4},{8,9},{9,10},{10,1... | collective-permute-start | bytes 405512 | tf_op jit(solution)/shard_map/ppermute | solution.py:50
  14.0 6.0 %collective-permute-start.2 = (bf16[1,132,1,512]{3,1,2,0:T(8,128)(2,1)S(1)}, bf16[1,132,1,512]{3,1,2,0:T(8,128)(2,1)S(1)}, u32[]{:S(2)}, u32[]{:S(2)}) collective-permute-start(bf16[1,132,1,512]{3,1,2,0:T(8,128)(2,1)S(1)} %bitcast.153), channel_id=1, source_target_pairs={{0,3},{1,0},{2,1},{3,2},{4,7},{5,4},{6,5},{7,6},{8,11},{9,8},{10,9... | collective-permute-start | bytes 405512 | tf_op jit(solution)/shard_map/ppermute | solution.py:50
  21.6 3.1 %copy-start.11 = (s32[128,8]{0,1:T(8,128)S(1)}, s32[128,8]{0,1:T(8,128)}, u32[]{:S(2)}) copy-start(s32[128,8]{0,1:T(8,128)} %param.7) | copy-start | bytes 12292
  23.7 40.7 %collective-permute-start.3 = (bf16[8,1,4,36,768]{4,0,3,2,1:T(8,128)(2,1)S(1)}, bf16[8,1,4,36,768]{4,0,3,2,1:T(8,128)(2,1)S(1)}, u32[]{:S(2)}, u32[]{:S(2)}) collective-permute-start(bf16[8,1,4,36,768]{4,0,3,2,1:T(8,128)(2,1)S(1)} %copy.217), channel_id=1, source_target_pairs={{0,2},{1,3},{2,0},{3,1},{4,6},{5,7},{6,4},{7,5},{8,10},{9,11},{10,... | collective-permute-start | bytes 5308424 | tf_op jit(solution)/shard_map/ppermute | solution.py:32
  64.4 2.4 %copy-start.2 = (bf16[8,1,4,36,768]{4,0,3,2,1:T(8,128)(2,1)}, bf16[8,1,4,36,768]{4,0,3,2,1:T(8,128)(2,1)S(1)}, u32[]{:S(2)}) copy-start(bf16[8,1,4,36,768]{4,0,3,2,1:T(8,128)(2,1)S(1)} %collective-permute-done.3) | copy-start | bytes 5308420
  66.7 33.7 %collective-permute-start.4 = (bf16[8,2,4,36,768]{4,0,3,2,1:T(8,128)(2,1)}, bf16[8,2,4,36,768]{4,0,3,2,1:T(8,128)(2,1)}, u32[]{:S(2)}, u32[]{:S(2)}) collective-permute-start(bf16[8,2,4,36,768]{4,0,3,2,1:T(8,128)(2,1)} %pad_maximum_fusion), channel_id=1, source_target_pairs={{0,1},{1,0},{2,3},{3,2},{4,5},{5,4},{6,7},{7,6},{8,9},{9,8},{10,11... | collective-permute-start | bytes 10616840 | tf_op jit(solution)/shard_map/ppermute | solution.py:33
  72.4 3.4 %copy-start = (bf16[4,4,132,512]{3,2,1,0:T(8,128)(2,1)}, bf16[4,4,132,512]{3,2,1,0:T(8,128)(2,1)S(1)}, u32[]{:S(2)}) copy-start(bf16[4,4,132,512]{3,2,1,0:T(8,128)(2,1)S(1)} %copy.211) | copy-start | bytes 6488068
  84.5 6.3 %copy-start.3 = (bf16[8,1,4,36,768]{4,0,3,2,1:T(8,128)(2,1)S(1)}, bf16[8,1,4,36,768]{4,0,3,2,1:T(8,128)(2,1)}, u32[]{:S(2)}) copy-start(bf16[8,1,4,36,768]{4,0,3,2,1:T(8,128)(2,1)} %copy-done.2) | copy-start | bytes 5308420
  84.5 6.3 %copy-start.9 = (bf16[4,1,8,36,512]{4,3,2,1,0:T(8,128)(2,1)S(1)}, bf16[4,1,8,36,512]{4,3,2,1,0:T(8,128)(2,1)}, u32[]{:S(2)}) copy-start(bf16[4,1,8,36,512]{4,3,2,1,0:T(8,128)(2,1)} %get-tuple-element.20) | copy-start | bytes 3538948
  90.8 5.0 %copy-start.5 = (bf16[8,1,4,36,768]{4,2,3,1,0:T(4,128)(2,1)S(1)}, bf16[8,1,4,36,768]{4,2,3,1,0:T(4,128)(2,1)}, u32[]{:S(2)}) copy-start(bf16[8,1,4,36,768]{4,2,3,1,0:T(4,128)(2,1)} %param.8) | copy-start | bytes 5308420
  90.8 5.0 %copy-start.8 = (bf16[4,1,8,36,512]{4,3,2,1,0:T(8,128)(2,1)S(1)}, bf16[4,1,8,36,512]{4,3,2,1,0:T(8,128)(2,1)}, u32[]{:S(2)}) copy-start(bf16[4,1,8,36,512]{4,3,2,1,0:T(8,128)(2,1)} %get-tuple-element.35) | copy-start | bytes 3538948
  90.8 12.0 %slice-start = ((s8[6291456]{0:T(1024)(128)(4,1)}), s8[2097152]{0:T(1024)(128)(4,1)S(1)}, s32[]{:S(2)}) async-start(s8[6291456]{0:T(1024)(128)(4,1)} %bitcast.161), calls=%async_computation.2 | async-start | bytes 4194304
  95.8 7.0 %slice-start.1 = ((s8[6291456]{0:T(1024)(128)(4,1)}), s8[4194304]{0:T(1024)(128)(4,1)S(1)}, s32[]{:S(2)}) async-start(s8[6291456]{0:T(1024)(128)(4,1)} %bitcast.161), calls=%async_computation.3 | async-start | bytes 8388608
  100.4 2.4 %copy-start.7 = (bf16[4,1,8,36,512]{4,3,2,1,0:T(8,128)(2,1)S(1)}, bf16[4,1,8,36,512]{4,3,2,1,0:T(8,128)(2,1)}, u32[]{:S(2)}) copy-start(bf16[4,1,8,36,512]{4,3,2,1,0:T(8,128)(2,1)} %get-tuple-element.18) | copy-start | bytes 3538948
  102.8 1.8 %copy-start.6 = (bf16[4,1,8,36,512]{4,3,2,1,0:T(8,128)(2,1)S(1)}, bf16[4,1,8,36,512]{4,3,2,1,0:T(8,128)(2,1)}, u32[]{:S(2)}) copy-start(bf16[4,1,8,36,512]{4,3,2,1,0:T(8,128)(2,1)} %get-tuple-element.19) | copy-start | bytes 3538948
  109.0 31.6 %all-to-all-start = ((f32[16,1,288]{2,1,0:T(1,128)}), f32[16,1,288]{2,1,0:T(1,128)}, u32[]{:S(2)}, u32[]{:S(2)}) async-start(f32[16,1,288]{2,1,0:T(1,128)} %reshape.86), calls=%async_computation | async-start | bytes 49152 | tf_op jit(solution)/shard_map/all_to_all | solution.py:99
  113.1 3.4 %copy-start.1 = (bf16[4,1,8,36,512]{4,3,2,1,0:T(8,128)(2,1)S(1)}, bf16[4,1,8,36,512]{4,3,2,1,0:T(8,128)(2,1)}, u32[]{:S(2)}) copy-start(bf16[4,1,8,36,512]{4,3,2,1,0:T(8,128)(2,1)} %get-tuple-element.37) | copy-start | bytes 3538948
  116.5 2.0 %copy-start.4 = (bf16[8,1,4,36,768]{4,0,3,2,1:T(8,128)(2,1)S(1)}, bf16[8,1,4,36,768]{4,0,3,2,1:T(8,128)(2,1)}, u32[]{:S(2)}) copy-start(bf16[8,1,4,36,768]{4,0,3,2,1:T(8,128)(2,1)} %copy-done.2) | copy-start | bytes 5308420
  127.9 14.8 %copy-start.10 = (pred[128,8,32]{0,2,1:T(8,128)(4,1)S(1)}, pred[128,8,32]{0,2,1:T(8,128)(4,1)}, u32[]{:S(2)}) copy-start(pred[128,8,32]{0,2,1:T(8,128)(4,1)} %get-tuple-element.34) | copy-start | bytes 98308
Sparse Core Ops, SparseCore 0:
  21.8 48.5 all-gather.1
